TPU v7x, 32 devices: a whole 2x2x4 slice. The times are simulated.
32 devices in a mesh: grp: 2 (over x), blk: 2 (over core), head: 8 (over z, y).
Axes of the slice: x: 2, y: 2, z: 4, core: 2. Of those that a mesh axis runs over, the one named last changes fastest.
Arguments:
- stream: bfloat16 [1024, 3072], P(('grp', 'blk', 'head')), parts along dimension 0, may hold values from -6 to 6
- gains: float32 [3, 3072], replicated, may hold values from 0.25 to 1.75
- dilations: int32 [2], replicated, may hold values from 1 to 64, as said below
- w_conv: bfloat16 [2, 3, 3072, 2, 3072], P(None, None, None, None, 'head'), may hold values from -0.0625 to 0.0625
- w_mix: bfloat16 [2, 3072, 3072], P(None, 'head'), may hold values from -0.109375 to 0.109375
- w_qkv: bfloat16 [3072, 3, 8, 128], P(None, None, 'head')
- w_out: bfloat16 [8, 128, 3072], P('head'), may hold values from -0.1875 to 0.1875
Outputs:
- mixed: bfloat16 [1024, 3072], P(('grp', 'blk', 'head')), parts along dimension 0
There are 2 independent parts, one for each index of `grp`. A program takes and returns all parts, laid end to end along the dimension named above; an argument that names none is the same for every part. Nothing has to cross between parts.
Inputs may be any that keep to these rules, and one draw needn't show every extreme that they name: `dilations`: each dilation is a whole number; one is exactly 64.
All inputs are finite; a program needn't handle non-finite values.
Results may differ from a plain program's by a relative error of at most 0.03.
Values may be sent and summed in bfloat16 or wider, within the bound.
No kernel may reach another device: no remote copies, remote signals or barrier semaphores. Data moves between devices by JAX's collectives and lax.ppermute only.
A program may use at most 128 MiB of HBM per device.

v0:
```python
import jax
import jax.numpy as jnp
from jax import lax
from jax.sharding import PartitionSpec as P

LARGEST_DILATION = 64


def shifted(value, axis, by):
    length = lax.axis_size(axis)
    pairs = [(i, i + by) for i in range(length) if 0 <= i + by < length]
    return lax.ppermute(value, axis, pairs)


def normed(values, gain):
    wide = values.astype(jnp.float32)
    scale = lax.rsqrt(jnp.mean(wide * wide, axis=-1, keepdims=True) + 1e-06)
    return (wide * scale * gain).astype(jnp.bfloat16)


def rounded_term(left, right):
    term = jnp.dot(left, right, preferred_element_type=jnp.float32)
    return lax.optimization_barrier(term.astype(jnp.bfloat16)).astype(jnp.float32)


def convolution_gate(hidden, kernel, dilation_factor):
    all_rows = hidden.shape[0]
    width = hidden.shape[1]
    own_width = kernel.shape[-1]
    border_rows = 2 * LARGEST_DILATION
    before = shifted(hidden[all_rows - border_rows :], "blk", 1)
    padded = jnp.concatenate([before, hidden], axis=0)
    pre_act = jnp.zeros((all_rows, 2 * own_width), jnp.float32)
    for tap_idx in range(3):
        start = border_rows - tap_idx * dilation_factor
        slab = lax.dynamic_slice_in_dim(padded, start, all_rows, 0)
        pre_act = pre_act + jnp.dot(
            slab, kernel[tap_idx].reshape(width, 2 * own_width), preferred_element_type=jnp.float32
        )
    return (jnp.tanh(pre_act[:, :own_width]) * jax.nn.sigmoid(pre_act[:, own_width:])).astype(
        jnp.bfloat16
    )


def conv_share(gated, weight, tok_rows):

    def term(start, count):
        return rounded_term(gated, weight)

    return lax.psum_scatter(
        term(jnp.int32(0), tok_rows * lax.axis_size("head")).astype(jnp.bfloat16),
        "head",
        scatter_dimension=0,
        tiled=True,
    ).astype(jnp.float32)


def attention_portion_for(heads_out, out_block, tok_rows):

    def term(start, count):
        return rounded_term(heads_out, out_block)

    return lax.psum_scatter(
        term(jnp.int32(0), tok_rows * lax.axis_size("head")).astype(jnp.bfloat16),
        "head",
        scatter_dimension=0,
        tiled=True,
    ).astype(jnp.float32)


def attend(queries, keys_in, values_in, causal):
    scale = queries.shape[1] ** (-0.5)
    scores = jnp.einsum("qd,kd->qk", queries, keys_in, preferred_element_type=jnp.float32) * scale
    if causal:
        rows_q = lax.broadcasted_iota(jnp.int32, scores.shape, 0)
        rows_k = lax.broadcasted_iota(jnp.int32, scores.shape, 1)
        scores = jnp.where(rows_q >= rows_k, scores, -1e30)
    peak = jnp.max(scores, axis=1)
    probs = jnp.exp(scores - peak[:, None])
    denom = jnp.sum(probs, axis=1)
    weighted = jnp.dot(probs.astype(jnp.bfloat16), values_in, preferred_element_type=jnp.float32)
    return (peak, denom, weighted)


def neutral(count, head_size):
    return (
        jnp.full((count,), -1e30, jnp.float32),
        jnp.zeros((count,), jnp.float32),
        jnp.zeros((count, head_size), jnp.float32),
    )


def combine(first, second):
    peak = jnp.maximum(first[0], second[0])
    scale_one = jnp.exp(first[0] - peak)
    scale_two = jnp.exp(second[0] - peak)
    denom = first[1] * scale_one + second[1] * scale_two
    weighted = first[2] * scale_one[:, None] + second[2] * scale_two[:, None]
    return (peak, denom, weighted)


def per_device(stream, gains, dilations, w_conv, w_mix, w_qkv, w_out):
    blk_pos = lax.axis_index("blk")
    tok_rows = stream.shape[0]
    width = stream.shape[1]
    head_size = w_qkv.shape[3]
    layers = w_conv.shape[0]
    qkv_weight = w_qkv.reshape(width, 3 * head_size)
    share = stream
    state = lax.all_gather(stream, "head", axis=0, tiled=True)
    for layer_idx in range(layers):
        gated = convolution_gate(
            normed(state, gains[layer_idx]), w_conv[layer_idx], dilations[layer_idx]
        )
        summed = conv_share(gated, w_mix[layer_idx], tok_rows)
        share = (share.astype(jnp.float32) + summed).astype(jnp.bfloat16)
        state = lax.all_gather(share, "head", axis=0, tiled=True)
    all_rows = state.shape[0]
    attn_in = normed(state, gains[layers])
    projected = jnp.dot(attn_in, qkv_weight, preferred_element_type=jnp.float32).astype(
        jnp.bfloat16
    )
    queries = projected[:, :head_size]
    keys_own = projected[:, head_size : 2 * head_size]
    values_own = projected[:, 2 * head_size :]
    keys_prev, values_prev = shifted((keys_own, values_own), "blk", 1)
    own_part = attend(queries, keys_own, values_own, True)
    crossing_portion = lax.cond(
        blk_pos > 0,
        lambda: attend(queries, keys_prev, values_prev, False),
        lambda: neutral(all_rows, head_size),
    )
    peak, denom, weighted = combine(own_part, crossing_portion)
    heads_out = (weighted / denom[:, None]).astype(jnp.bfloat16)
    attn_share = attention_portion_for(heads_out, w_out[0], tok_rows)
    return (share.astype(jnp.float32) + attn_share).astype(jnp.bfloat16)


def solution(mesh):
    placed = (
        P(("grp", "blk", "head"), None),
        P(),
        P(),
        P(None, None, None, None, "head"),
        P(None, "head", None),
        P(None, None, "head", None),
        P("head", None, None),
    )
    return jax.shard_map(
        per_device,
        mesh=mesh,
        in_specs=placed,
        out_specs=P(("grp", "blk", "head"), None),
        check_vma=False,
    )
```

profile of v0, /device:TPU:0, one launch (start us, length us, event | category | flops | bytes accessed | tf_op | source)
XLA Modules:
  0.0 449.6 jit_solution(16338248343998651655)
XLA Ops:
  8.3 48.2 %all-gather.4.cloned.1.call-done = bf16[256,3072]{1,0:T(8,128)(2,1)} async-done(((bf16[32,3072]{1,0:T(8,128)(2,1)}), bf16[256,3072]{1,0:T(8,128)(2,1)}) %all-gather.4.cloned.1.call-update) | async-done | bytes 1572880 | tf_op jit(solution)/shard_map/all_gather | solution.py:110
  62.4 22.4 %fusion.95 = (bf16[1,1,3072,2,384]{4,3,2,1,0:T(2,128)(2,1)}, bf16[1,1,3072,2,384]{4,3,2,1,0:T(2,128)(2,1)}, bf16[1,1,3072,2,384]{4,3,2,1,0:T(2,128)(2,1)S(1)}, b...) fusion(bf16[2,3,3072,2,384]{4,3,2,1,0:T(2,128)(2,1)} %param.12), kind=kLoop, calls=%fused_computation.106 | loop fusion | bytes 56623104 | tf_op jit(solution)/shard_map/slice | solution.py:38
  87.4 3.0 copy.11
  90.4 3.0 copy.9
  93.4 3.1 copy.10
  96.5 3.9 fusion.100
  100.4 4.4 fusion.25
  104.9 2.9 fusion.37
  107.8 2.2 convolution_convert_fusion.2
  110.1 64.3 %reduce-scatter.4.cloned.1.call-done = bf16[32,3072]{1,0:T(8,128)(2,1)} async-done(((bf16[256,3072]{1,0:T(8,128)(2,1)}), bf16[32,3072]{1,0:T(8,128)(2,1)}) %reduce-scatter.4.cloned.1.call-update) | async-done | bytes 196624 | tf_op jit(solution)/shard_map/reduce_scatter | solution.py:50
  176.1 43.9 %all-gather.6.cloned.1.call-done = bf16[256,3072]{1,0:T(8,128)(2,1)} async-done(((bf16[32,3072]{1,0:T(8,128)(2,1)}), bf16[256,3072]{1,0:T(8,128)(2,1)}) %all-gather.6.cloned.1.call-update) | async-done | bytes 1572880 | tf_op jit(solution)/shard_map/all_gather | solution.py:117
  223.7 2.2 collective-permute-start.1
  227.8 5.3 %copy.14 = bf16[384,8,2,384]{3,1,2,0:T(8,128)(2,1)} copy(bf16[384,8,2,384]{3,2,1,0:T(2,128)(2,1)} %bitcast.55) | data formatting | bytes 9437184
  233.1 5.5 %copy.12 = bf16[384,8,2,384]{3,1,2,0:T(8,128)(2,1)} copy(bf16[384,8,2,384]{3,2,1,0:T(2,128)(2,1)} %bitcast.54) | data formatting | bytes 9437184
  238.6 3.0 copy.13
  241.7 3.9 fusion.101
  245.6 2.9 fusion.19
  248.5 2.7 fusion.43
  251.2 2.2 convolution_convert_fusion.1
  253.5 64.3 %reduce-scatter.6.cloned.1.call-done = bf16[32,3072]{1,0:T(8,128)(2,1)} async-done(((bf16[256,3072]{1,0:T(8,128)(2,1)}), bf16[32,3072]{1,0:T(8,128)(2,1)}) %reduce-scatter.6.cloned.1.call-update) | async-done | bytes 196624 | tf_op jit(solution)/shard_map/reduce_scatter | solution.py:50
  319.6 2.5 copy.8
  322.1 40.9 %all-gather.8.cloned.1.call-done = bf16[256,3072]{1,0:T(8,128)(2,1)} async-done(((bf16[32,3072]{1,0:T(8,128)(2,1)}), bf16[256,3072]{1,0:T(8,128)(2,1)}) %all-gather.8.cloned.1.call-update) | async-done | bytes 1572880 | tf_op jit(solution)/shard_map/all_gather | solution.py:117
  364.8 3.2 fusion.46
  375.0 66.2 %reduce-scatter.8.cloned.1.call-done = bf16[32,3072]{1,0:T(8,128)(2,1)} async-done(((bf16[256,3072]{1,0:T(8,128)(2,1)}), bf16[32,3072]{1,0:T(8,128)(2,1)}) %reduce-scatter.8.cloned.1.call-update) | async-done | bytes 196624 | tf_op jit(solution)/shard_map/reduce_scatter | solution.py:63
  (82 shorter events, 26.7 us)
Async XLA Ops:
  6.5 366.5 %copy-start = (bf16[1,128,3072]{2,1,0:T(8,128)(2,1)S(1)}, bf16[1,128,3072]{2,1,0:T(8,128)(2,1)}, u32[]{:S(2)}) copy-start(bf16[1,128,3072]{2,1,0:T(8,128)(2,1)} %param.15) | copy-start | bytes 2359300
  6.5 49.9 %all-gather.4.cloned.1.call-start = ((), (), s32[]{:S(2)}) async-start(), calls=%async_computation.3 | async-start | bytes 1769472 | tf_op jit(solution)/shard_map/all_gather | solution.py:110
  7.3 167.1 %reduce-scatter.4.cloned.1.call-start = ((), (), s32[]{:S(2)}) async-start(), calls=%async_computation.4 | async-start | bytes 1769472 | tf_op jit(solution)/shard_map/reduce_scatter | solution.py:50
  60.2 24.6 %copy-start.6 = (s32[2]{0:T(128)S(1)}, s32[2]{0:T(128)}, u32[]{:S(2)}) copy-start(s32[2]{0:T(128)} %param.11) | copy-start | bytes 28
  60.3 40.1 %collective-permute-start = (bf16[128,3072]{1,0:T(8,128)(2,1)S(1)}, bf16[128,3072]{1,0:T(8,128)(2,1)}, u32[]{:S(2)}, u32[]{:S(2)}) collective-permute-start(bf16[128,3072]{1,0:T(8,128)(2,1)S(1)} %slice.102), channel_id=1, source_target_pairs={{0,8},{1,9},{2,10},{3,11},{4,12},{5,13},{6,14},{7,15},{16,24},{17,... | collective-permute-start | bytes 2359304 | tf_op jit(solution)/shard_map/ppermute | solution.py:12
  96.5 8.3 %slice-start.2 = ((s8[4718592]{0:T(1024)(128)(4,1)}), s8[4194304]{0:T(1024)(128)(4,1)S(1)}, s32[]{:S(2)}) async-start(s8[4718592]{0:T(1024)(128)(4,1)} %bitcast.59), calls=%async_computation.11 | async-start | bytes 8388608
  100.4 4.5 slice-start.3
  100.4 7.4 %slice-start.6 = ((s8[4718592]{0:T(1024)(128)(4,1)}), s8[4194304]{0:T(1024)(128)(4,1)S(1)}, s32[]{:S(2)}) async-start(s8[4718592]{0:T(1024)(128)(4,1)} %bitcast.73), calls=%async_computation.15 | async-start | bytes 8388608
  107.8 66.6 %copy-start.5 = (bf16[32,3072]{1,0:T(8,128)(2,1)S(1)}, bf16[32,3072]{1,0:T(8,128)(2,1)}, u32[]{:S(2)}) copy-start(bf16[32,3072]{1,0:T(8,128)(2,1)} %param.9) | copy-start | bytes 589828
  110.0 109.9 %all-gather.6.cloned.1.call-start = ((), (), s32[]{:S(2)}) async-start(), calls=%async_computation.5 | async-start | bytes 1769472 | tf_op jit(solution)/shard_map/all_gather | solution.py:117
  176.0 141.8 %reduce-scatter.6.cloned.1.call-start = ((), (), s32[]{:S(2)}) async-start(), calls=%async_computation.6 | async-start | bytes 1769472 | tf_op jit(solution)/shard_map/reduce_scatter | solution.py:50
  223.7 21.8 %collective-permute-start.1 = (bf16[128,3072]{1,0:T(8,128)(2,1)S(1)}, bf16[128,3072]{1,0:T(8,128)(2,1)}, u32[]{:S(2)}, u32[]{:S(2)}) collective-permute-start(bf16[128,3072]{1,0:T(8,128)(2,1)S(1)} %slice.105), channel_id=1, source_target_pairs={{0,8},{1,9},{2,10},{3,11},{4,12},{5,13},{6,14},{7,15},{16,24},{17,... | collective-permute-start | bytes 2359304 | tf_op jit(solution)/shard_map/ppermute | solution.py:12
  233.1 5.5 %slice-start = ((s8[4718592]{0:T(1024)(128)(4,1)}), s8[4194304]{0:T(1024)(128)(4,1)S(1)}, s32[]{:S(2)}) async-start(s8[4718592]{0:T(1024)(128)(4,1)} %bitcast.51), calls=%async_computation.9 | async-start | bytes 8388608
  233.1 5.5 %slice-start.1 = ((s8[4718592]{0:T(1024)(128)(4,1)}), s8[524288]{0:T(1024)(128)(4,1)S(1)}, s32[]{:S(2)}) async-start(s8[4718592]{0:T(1024)(128)(4,1)} %bitcast.51), calls=%async_computation.10 | async-start | bytes 1048576
  241.6 3.9 copy-start.1
  241.7 6.8 %slice-start.4 = ((s8[4718592]{0:T(1024)(128)(4,1)}), s8[4194304]{0:T(1024)(128)(4,1)S(1)}, s32[]{:S(2)}) async-start(s8[4718592]{0:T(1024)(128)(4,1)} %bitcast.64), calls=%async_computation.13 | async-start | bytes 8388608
  245.6 5.6 %slice-start.8 = ((s8[4718592]{0:T(1024)(128)(4,1)}), s8[4194304]{0:T(1024)(128)(4,1)S(1)}, s32[]{:S(2)}) async-start(s8[4718592]{0:T(1024)(128)(4,1)} %bitcast.75), calls=%async_computation.17 | async-start | bytes 8388608
  251.2 66.6 %copy-start.4 = (bf16[32,3072]{1,0:T(8,128)(2,1)S(1)}, bf16[32,3072]{1,0:T(8,128)(2,1)}, u32[]{:S(2)}) copy-start(bf16[32,3072]{1,0:T(8,128)(2,1)} %add_convert_fusion.2) | copy-start | bytes 589828
  251.2 68.3 %copy-start.2 = (bf16[3072,3,1,128]{3,0,2,1:T(8,128)(2,1)S(1)}, bf16[3072,3,1,128]{3,0,2,1:T(8,128)(2,1)}, u32[]{:S(2)}) copy-start(bf16[3072,3,1,128]{3,0,2,1:T(8,128)(2,1)} %param.14) | copy-start | bytes 7077892
  253.5 109.5 %all-gather.8.cloned.1.call-start = ((), (), s32[]{:S(2)}) async-start(), calls=%async_computation.7 | async-start | bytes 1769472 | tf_op jit(solution)/shard_map/all_gather | solution.py:117
  319.5 121.6 %reduce-scatter.8.cloned.1.call-start = ((), (), s32[]{:S(2)}) async-start(), calls=%async_computation.8 | async-start | bytes 1769472 | tf_op jit(solution)/shard_map/reduce_scatter | solution.py:63
  368.0 73.1 %copy-start.3 = (bf16[32,3072]{1,0:T(8,128)(2,1)S(1)}, bf16[32,3072]{1,0:T(8,128)(2,1)}, u32[]{:S(2)}) copy-start(bf16[32,3072]{1,0:T(8,128)(2,1)} %add_convert_fusion.1) | copy-start | bytes 589828
  368.2 2.7 collective-permute-start.2
  369.5 2.2 collective-permute-start.3
  (3 other events, 8.5 us)
Sparse Core Ops, SparseCore 0:
  9.5 46.8 all-gather.3
  110.1 64.1 reduce-scatter.3
  176.8 43.1 all-gather.5
  253.6 64.1 reduce-scatter.5
  319.9 43.0 all-gather.7
  375.1 65.9 reduce-scatter.7
where the time goes:
time: 450 us
  waiting for transfers between devices  329 us (73%)
  local copies, waits for them, and re-layouts  50.2 us (11%)
  matrix products  30.3 us (7%)
  between operations  17.7 us (4%)
  other arithmetic  14.9 us (3%)
  starting transfers between devices  7.17 us (2%)
    reduce_scatter x2, waiting for transfers between devices, conv_share(): lax.psum_scatter(term(jnp.int32(0), tok_rows * lax.axis_size('head')).ast...  129 us
    all_gather x2, waiting for transfers between devices, per_device(): state = lax.all_gather(share, 'head', axis=0, tiled=True)  84.8 us
    reduce_scatter x1, waiting for transfers between devices, attention_portion_for(): lax.psum_scatter(term(jnp.int32(0), tok_rows * lax.axis_size('head')).ast...  66.2 us
    all_gather x1, waiting for transfers between devices, per_device(): state = lax.all_gather(stream, 'head', axis=0, tiled=True)  48.2 us
    unnamed x41, local copies, waits for them, and re-layouts  25.5 us
    slice x1, local copies, waits for them, and re-layouts, convolution_gate(): kernel[tap_idx].reshape(width, 2 * own_width)  22.4 us
    dot_general x6, matrix products, convolution_gate(): jnp.dot(slab, kernel[tap_idx].reshape(width, 2 * own_width), preferred_el...  20.6 us
  transfers between devices with their start and end apart: 10, of which 7 were waited for; matrix products, arithmetic and copies ran while one was open for 13% of the time, Pallas kernels for 0%

commit v1 on v0

--- a/solution.py
+++ b/solution.py
@@ -107,7 +107,16 @@
     layers = w_conv.shape[0]
     qkv_weight = w_qkv.reshape(width, 3 * head_size)
     share = stream
-    state = lax.all_gather(stream, "head", axis=0, tiled=True)
+    answer, carry_out = (lax.axis_size("head"), lax.axis_index("head"))
+    state, item_now = (stream, 1)
+    while item_now < answer:
+        g_now = lax.ppermute(
+            state, axis_name="head", perm=tuple(((u, u ^ item_now) for u in range(answer)))
+        )
+        latest = jnp.concatenate([state, g_now], axis=0)
+        even = jnp.concatenate([g_now, state], axis=0)
+        state = jnp.where(carry_out & item_now == 0, latest, even)
+        item_now = 2 * item_now
     for layer_idx in range(layers):
         gated = convolution_gate(
             normed(state, gains[layer_idx]), w_conv[layer_idx], dilations[layer_idx]

time: 450 us -> 468 us (1.040)
  local copies, waits for them, and re-layouts: 50.2 us -> 61.1 us
  starting transfers between devices: 7.17 us -> 14.7 us
    all_gather x1 -> x0, waiting for transfers between devices: 48.2 us -> none  [per_device(): state = lax.all_gather(stream, 'head', axis=0, tiled=True)]
    ppermute x0 -> x3, waiting for transfers between devices: none -> 45.7 us  [per_device(): lax.ppermute(state, axis_name='head', perm=tuple(((u, u ^ item_now) for u...]
    ppermute x0 -> x3, starting transfers between devices: none -> 7.39 us  [per_device(): lax.ppermute(state, axis_name='head', perm=tuple(((u, u ^ item_now) for u...]
    unnamed x41 -> x43, local copies, waits for them, and re-layouts: 25.5 us -> 32.7 us
  transfers between devices with their start and end apart: 10 -> 12, of which waited for: 7 -> 9; matrix products, arithmetic and copies ran while one was open for 13% -> 15% of each run, Pallas kernels for 0% -> 0%
where the time goes in v1:
time: 468 us; the launch traced here: 467 us
  waiting for transfers between devices  328 us (70%)
  local copies, waits for them, and re-layouts  61.1 us (13%)
  matrix products  30.3 us (6%)
  between operations  17.5 us (4%)
  other arithmetic  15.2 us (3%)
  starting transfers between devices  14.7 us (3%)
    reduce_scatter x2, waiting for transfers between devices, conv_share(): lax.psum_scatter(term(jnp.int32(0), tok_rows * lax.axis_size('head')).ast...  131 us
    all_gather x2, waiting for transfers between devices, per_device(): state = lax.all_gather(share, 'head', axis=0, tiled=True)  84.8 us
    reduce_scatter x1, waiting for transfers between devices, attention_portion_for(): lax.psum_scatter(term(jnp.int32(0), tok_rows * lax.axis_size('head')).ast...  66.1 us
    ppermute x3, waiting for transfers between devices, per_device(): lax.ppermute(state, axis_name='head', perm=tuple(((u, u ^ item_now) for u...  45.7 us
    unnamed x43, local copies, waits for them, and re-layouts  32.7 us
    slice x1, local copies, waits for them, and re-layouts, convolution_gate(): kernel[tap_idx].reshape(width, 2 * own_width)  26.1 us
    dot_general x6, matrix products, convolution_gate(): jnp.dot(slab, kernel[tap_idx].reshape(width, 2 * own_width), preferred_el...  20.6 us
  transfers between devices with their start and end apart: 12, of which 9 were waited for; matrix products, arithmetic and copies ran while one was open for 15% of the time, Pallas kernels for 0%

profile of v1, /device:TPU:0, one launch (start us, length us, event | category | flops | bytes accessed | tf_op | source)
XLA Modules:
  0.0 467.0 jit_solution(15174554862285761966)
XLA Ops:
  6.5 3.0 collective-permute-start
  9.5 5.1 %collective-permute-done = bf16[32,3072]{1,0:T(8,128)(2,1)S(1)} collective-permute-done((bf16[32,3072]{1,0:T(8,128)(2,1)}, bf16[32,3072]{1,0:T(8,128)(2,1)S(1)}, u32[]{:S(2)}, u32[]{:S(2)}) %collective-permute-start) | collective-permute-done | bytes 196640 | tf_op jit(solution)/shard_map/ppermute | solution.py:113
  17.6 8.5 %collective-permute-done.1 = bf16[64,3072]{1,0:T(8,128)(2,1)S(1)} collective-permute-done((bf16[64,3072]{1,0:T(8,128)(2,1)S(1)}, bf16[64,3072]{1,0:T(8,128)(2,1)S(1)}, u32[]{:S(2)}, u32[]{:S(2)}) %collective-permute-start.1) | collective-permute-done | bytes 393248 | tf_op jit(solution)/shard_map/ppermute | solution.py:113
  26.2 2.6 collective-permute-start.2
  29.8 32.1 %collective-permute-done.2 = bf16[128,3072]{1,0:T(8,128)(2,1)S(1)} collective-permute-done((bf16[128,3072]{1,0:T(8,128)(2,1)S(1)}, bf16[128,3072]{1,0:T(8,128)(2,1)S(1)}, u32[]{:S(2)}, u32[]{:S(2)}) %collective-permute-start.2) | collective-permute-done | bytes 786464 | tf_op jit(solution)/shard_map/ppermute | solution.py:113
  67.2 26.1 %fusion.91 = (bf16[1,1,3072,2,384]{4,3,2,1,0:T(2,128)(2,1)}, bf16[1,1,3072,2,384]{4,3,2,1,0:T(2,128)(2,1)}, bf16[1,1,3072,2,384]{4,3,2,1,0:T(2,128)(2,1)}, bf16[...) fusion(bf16[2,3,3072,2,384]{4,3,2,1,0:T(2,128)(2,1)} %param.12), kind=kLoop, calls=%fused_computation.108 | loop fusion | bytes 56623104 | tf_op jit(solution)/shard_map/slice | solution.py:38
  96.0 5.4 %copy.10 = bf16[384,8,2,384]{3,1,2,0:T(8,128)(2,1)} copy(bf16[384,8,2,384]{3,2,1,0:T(2,128)(2,1)} %bitcast.58) | data formatting | bytes 9437184
  101.4 3.0 copy.9
  104.5 5.3 %copy.11 = bf16[384,8,2,384]{3,1,2,0:T(8,128)(2,1)} copy(bf16[384,8,2,384]{3,2,1,0:T(2,128)(2,1)} %bitcast.54) | data formatting | bytes 9437184
  109.8 3.9 fusion.96
  113.7 3.0 fusion.28
  116.7 2.9 add_add_fusion
  122.0 66.4 %reduce-scatter.4.cloned.1.call-done = bf16[32,3072]{1,0:T(8,128)(2,1)} async-done(((bf16[256,3072]{1,0:T(8,128)(2,1)}), bf16[32,3072]{1,0:T(8,128)(2,1)}) %reduce-scatter.4.cloned.1.call-update) | async-done | bytes 196624 | tf_op jit(solution)/shard_map/reduce_scatter | solution.py:50
  190.2 43.8 %all-gather.3.cloned.1.call-done = bf16[256,3072]{1,0:T(8,128)(2,1)} async-done(((bf16[32,3072]{1,0:T(8,128)(2,1)}), bf16[256,3072]{1,0:T(8,128)(2,1)}) %all-gather.3.cloned.1.call-update) | async-done | bytes 1572880 | tf_op jit(solution)/shard_map/all_gather | solution.py:126
  242.0 5.3 %copy.12 = bf16[384,8,2,384]{3,1,2,0:T(8,128)(2,1)} copy(bf16[384,8,2,384]{3,2,1,0:T(2,128)(2,1)} %bitcast.53) | data formatting | bytes 9437184
  247.3 5.4 %copy.14 = bf16[384,8,2,384]{3,1,2,0:T(8,128)(2,1)} copy(bf16[384,8,2,384]{3,2,1,0:T(2,128)(2,1)} %bitcast.52) | data formatting | bytes 9437184
  252.7 5.3 %copy.13 = bf16[384,8,2,384]{3,1,2,0:T(8,128)(2,1)} copy(bf16[384,8,2,384]{3,2,1,0:T(2,128)(2,1)} %bitcast.51) | data formatting | bytes 9437184
  258.0 3.9 fusion.97
  261.9 4.2 fusion.19
  266.2 2.7 fusion.37
  271.2 64.2 %reduce-scatter.6.cloned.1.call-done = bf16[32,3072]{1,0:T(8,128)(2,1)} async-done(((bf16[256,3072]{1,0:T(8,128)(2,1)}), bf16[32,3072]{1,0:T(8,128)(2,1)}) %reduce-scatter.6.cloned.1.call-update) | async-done | bytes 196624 | tf_op jit(solution)/shard_map/reduce_scatter | solution.py:50
  339.7 41.0 %all-gather.5.cloned.1.call-done = bf16[256,3072]{1,0:T(8,128)(2,1)} async-done(((bf16[32,3072]{1,0:T(8,128)(2,1)}), bf16[256,3072]{1,0:T(8,128)(2,1)}) %all-gather.5.cloned.1.call-update) | async-done | bytes 1572880 | tf_op jit(solution)/shard_map/all_gather | solution.py:126
  382.5 3.2 fusion.40
  392.8 66.1 %reduce-scatter.8.cloned.1.call-done = bf16[32,3072]{1,0:T(8,128)(2,1)} async-done(((bf16[256,3072]{1,0:T(8,128)(2,1)}), bf16[32,3072]{1,0:T(8,128)(2,1)}) %reduce-scatter.8.cloned.1.call-update) | async-done | bytes 196624 | tf_op jit(solution)/shard_map/reduce_scatter | solution.py:63
  (89 shorter events, 37.6 us)
Async XLA Ops:
  6.5 384.3 %copy-start = (bf16[1,128,3072]{2,1,0:T(8,128)(2,1)S(1)}, bf16[1,128,3072]{2,1,0:T(8,128)(2,1)}, u32[]{:S(2)}) copy-start(bf16[1,128,3072]{2,1,0:T(8,128)(2,1)} %param.15) | copy-start | bytes 2359300
  6.5 181.9 %reduce-scatter.4.cloned.1.call-start = ((), (), s32[]{:S(2)}) async-start(), calls=%async_computation.3 | async-start | bytes 1769472 | tf_op jit(solution)/shard_map/reduce_scatter | solution.py:50
  6.5 8.1 %collective-permute-start = (bf16[32,3072]{1,0:T(8,128)(2,1)}, bf16[32,3072]{1,0:T(8,128)(2,1)S(1)}, u32[]{:S(2)}, u32[]{:S(2)}) collective-permute-start(bf16[32,3072]{1,0:T(8,128)(2,1)} %param.9), channel_id=1, source_target_pairs={{0,1},{1,0},{2,3},{3,2},{4,5},{5,4},{6,7},{7,6},{8,9},{9,8},{10,11... | collective-permute-start | bytes 589832 | tf_op jit(solution)/shard_map/ppermute | solution.py:113
  15.7 10.4 %collective-permute-start.1 = (bf16[64,3072]{1,0:T(8,128)(2,1)S(1)}, bf16[64,3072]{1,0:T(8,128)(2,1)S(1)}, u32[]{:S(2)}, u32[]{:S(2)}) collective-permute-start(bf16[64,3072]{1,0:T(8,128)(2,1)S(1)} %maximum_select_fusion.2), channel_id=1, source_target_pairs={{0,2},{1,3},{2,0},{3,1},{4,6},{5,7},{6,4},{7,5},{8,10},{9,11},{10,... | collective-permute-start | bytes 1179656 | tf_op jit(solution)/shard_map/ppermute | solution.py:113
  26.2 35.6 %collective-permute-start.2 = (bf16[128,3072]{1,0:T(8,128)(2,1)S(1)}, bf16[128,3072]{1,0:T(8,128)(2,1)S(1)}, u32[]{:S(2)}, u32[]{:S(2)}) collective-permute-start(bf16[128,3072]{1,0:T(8,128)(2,1)S(1)} %maximum_select_fusion.1), channel_id=1, source_target_pairs={{0,4},{1,5},{2,6},{3,7},{4,0},{5,1},{6,2},{7,3},{8,12},{9,13},{10,... | collective-permute-start | bytes 2359304 | tf_op jit(solution)/shard_map/ppermute | solution.py:113
  65.0 28.3 %copy-start.7 = (s32[2]{0:T(128)S(1)}, s32[2]{0:T(128)}, u32[]{:S(2)}) copy-start(s32[2]{0:T(128)} %param.11) | copy-start | bytes 28
  65.0 48.6 %collective-permute-start.3 = (bf16[128,3072]{1,0:T(8,128)(2,1)S(1)}, bf16[128,3072]{1,0:T(8,128)(2,1)}, u32[]{:S(2)}, u32[]{:S(2)}) collective-permute-start(bf16[128,3072]{1,0:T(8,128)(2,1)S(1)} %slice.102), channel_id=1, source_target_pairs={{0,8},{1,9},{2,10},{3,11},{4,12},{5,13},{6,14},{7,15},{16,24},{17,... | collective-permute-start | bytes 2359304 | tf_op jit(solution)/shard_map/ppermute | solution.py:12
  96.0 5.4 %slice-start = ((s8[4718592]{0:T(1024)(128)(4,1)}), s8[4194304]{0:T(1024)(128)(4,1)S(1)}, s32[]{:S(2)}) async-start(s8[4718592]{0:T(1024)(128)(4,1)} %bitcast.55), calls=%async_computation.8 | async-start | bytes 8388608
  96.0 5.4 %slice-start.1 = ((s8[4718592]{0:T(1024)(128)(4,1)}), s8[524288]{0:T(1024)(128)(4,1)S(1)}, s32[]{:S(2)}) async-start(s8[4718592]{0:T(1024)(128)(4,1)} %bitcast.55), calls=%async_computation.9 | async-start | bytes 1048576
  109.8 6.9 %slice-start.2 = ((s8[4718592]{0:T(1024)(128)(4,1)}), s8[4194304]{0:T(1024)(128)(4,1)S(1)}, s32[]{:S(2)}) async-start(s8[4718592]{0:T(1024)(128)(4,1)} %bitcast.60), calls=%async_computation.10 | async-start | bytes 8388608
  113.7 6.0 %slice-start.6 = ((s8[4718592]{0:T(1024)(128)(4,1)}), s8[4194304]{0:T(1024)(128)(4,1)S(1)}, s32[]{:S(2)}) async-start(s8[4718592]{0:T(1024)(128)(4,1)} %bitcast.73), calls=%async_computation.14 | async-start | bytes 8388608
  119.7 68.7 %copy-start.6 = (bf16[32,3072]{1,0:T(8,128)(2,1)S(1)}, bf16[32,3072]{1,0:T(8,128)(2,1)}, u32[]{:S(2)}) copy-start(bf16[32,3072]{1,0:T(8,128)(2,1)} %param.9) | copy-start | bytes 589828
  122.0 112.0 %all-gather.3.cloned.1.call-start = ((), (), s32[]{:S(2)}) async-start(), calls=%async_computation.4 | async-start | bytes 1769472 | tf_op jit(solution)/shard_map/all_gather | solution.py:126
  190.1 145.4 %reduce-scatter.6.cloned.1.call-start = ((), (), s32[]{:S(2)}) async-start(), calls=%async_computation.5 | async-start | bytes 1769472 | tf_op jit(solution)/shard_map/reduce_scatter | solution.py:50
  237.8 24.1 %collective-permute-start.4 = (bf16[128,3072]{1,0:T(8,128)(2,1)S(1)}, bf16[128,3072]{1,0:T(8,128)(2,1)}, u32[]{:S(2)}, u32[]{:S(2)}) collective-permute-start(bf16[128,3072]{1,0:T(8,128)(2,1)S(1)} %slice.105), channel_id=1, source_target_pairs={{0,8},{1,9},{2,10},{3,11},{4,12},{5,13},{6,14},{7,15},{16,24},{17,... | collective-permute-start | bytes 2359304 | tf_op jit(solution)/shard_map/ppermute | solution.py:12
  258.0 8.2 %slice-start.4 = ((s8[4718592]{0:T(1024)(128)(4,1)}), s8[4194304]{0:T(1024)(128)(4,1)S(1)}, s32[]{:S(2)}) async-start(s8[4718592]{0:T(1024)(128)(4,1)} %bitcast.63), calls=%async_computation.12 | async-start | bytes 8388608
  261.9 7.0 %slice-start.8 = ((s8[4718592]{0:T(1024)(128)(4,1)}), s8[4194304]{0:T(1024)(128)(4,1)S(1)}, s32[]{:S(2)}) async-start(s8[4718592]{0:T(1024)(128)(4,1)} %bitcast.75), calls=%async_computation.16 | async-start | bytes 8388608
  268.9 66.6 %copy-start.5 = (bf16[32,3072]{1,0:T(8,128)(2,1)S(1)}, bf16[32,3072]{1,0:T(8,128)(2,1)}, u32[]{:S(2)}) copy-start(bf16[32,3072]{1,0:T(8,128)(2,1)} %add_convert_fusion.2) | copy-start | bytes 589828
  268.9 68.3 %copy-start.3 = (bf16[3072,3,1,128]{3,0,2,1:T(8,128)(2,1)S(1)}, bf16[3072,3,1,128]{3,0,2,1:T(8,128)(2,1)}, u32[]{:S(2)}) copy-start(bf16[3072,3,1,128]{3,0,2,1:T(8,128)(2,1)} %param.14) | copy-start | bytes 7077892
  271.2 109.5 %all-gather.5.cloned.1.call-start = ((), (), s32[]{:S(2)}) async-start(), calls=%async_computation.6 | async-start | bytes 1769472 | tf_op jit(solution)/shard_map/all_gather | solution.py:126
  337.1 121.7 %reduce-scatter.8.cloned.1.call-start = ((), (), s32[]{:S(2)}) async-start(), calls=%async_computation.7 | async-start | bytes 1769472 | tf_op jit(solution)/shard_map/reduce_scatter | solution.py:63
  385.9 72.9 %copy-start.4 = (bf16[32,3072]{1,0:T(8,128)(2,1)S(1)}, bf16[32,3072]{1,0:T(8,128)(2,1)}, u32[]{:S(2)}) copy-start(bf16[32,3072]{1,0:T(8,128)(2,1)} %add_convert_fusion.1) | copy-start | bytes 589828
  385.9 2.8 collective-permute-start.5
  387.4 2.2 collective-permute-start.6
  (6 other events, 17.8 us)
Sparse Core Ops, SparseCore 0:
  122.1 66.2 reduce-scatter.3
  190.8 43.1 all-gather.2
  271.3 64.1 reduce-scatter.5
  337.5 43.1 all-gather.4
  392.9 65.9 reduce-scatter.7
